TPU v7x, 128 devices: a whole 4x4x4 slice. The times are simulated.
128 devices in a mesh: grains: 128 (over z, x, y, core).
Axes of the slice: x: 4, y: 4, z: 4, core: 2. Of those that a mesh axis runs over, the one named last changes fastest.
Arguments:
- tangent: float32 [8192, 128, 128], P('grains'), may hold values from -48 to 48
- blocks: bfloat16 [8192, 8, 128, 128], P('grains'), may hold values from -0.1875 to 0.1875
- columns: int32 [8192, 8], P('grains'), may hold values from 0 to 95, as said below
- counts: int32 [128], P('grains'), may hold values from 32 to 64, as said below
- send_lists: int32 [128, 2, 16], P('grains'), may hold values from 0 to 63, as said below
Outputs:
- basis: float32 [8192, 128, 128], P('grains')
- r_factor: float32 [128, 128], replicated
Inputs may be any that keep to these rules, and one draw needn't show every extreme that they name: `counts`: some device has exactly 64 live block rows; every device has at least 32. Every entry of send_lists[d] is below counts[d]. For block row b of device d, columns[., 0] is b; every other entry is below counts[d] or lies in 64 to 64 + 2 * 16 - 1 (received rows). Entries of slots that are not live follow the same law.
All inputs are finite; a program needn't handle non-finite values.
Results may differ from a plain program's by a relative error of at most 0.0028.
Values may be sent and summed in bfloat16 or wider, within the bound.
No kernel may reach another device: no remote copies, remote signals or barrier semaphores. Data moves between devices by JAX's collectives and lax.ppermute only.
A program may use at most 128 MiB of HBM per device.

v0:
```python
import jax
import jax.numpy as jnp
from jax import lax
from jax.sharding import PartitionSpec as P

SUBSTEPS = 3


def passed_along(shard, axis, by):
    length = lax.axis_size(axis)
    return lax.ppermute(shard, axis, [(i, (i + by) % length) for i in range(length)])


def apply_inverse(matrix, lower):
    return lax.linalg.triangular_solve(lower, matrix, left_side=False, lower=True, transpose_a=True)


def local(tangent, blocks, columns, counts, send_lists):
    slots, width, vectors = tangent.shape
    live = (jnp.arange(slots, dtype=jnp.int32) < counts[0]).astype(jnp.float32)[:, None, None]
    state = tangent * live
    for step in range(SUBSTEPS):
        rounded = state.astype(jnp.bfloat16)
        to_lower = rounded[send_lists[0, 0]]
        to_upper = rounded[send_lists[0, 1]]
        from_lower = passed_along(to_upper, "grains", 1)
        from_upper = passed_along(to_lower, "grains", -1)
        extended = jnp.concatenate([rounded, from_lower, from_upper], axis=0)
        gathered = extended[columns]
        update = jnp.einsum("bkij,bkjv->biv", blocks, gathered, preferred_element_type=jnp.float32)
        state = state + update * live
    flat = state.reshape(slots * width, vectors)
    first_low = jnp.linalg.cholesky(
        lax.psum(jnp.einsum("rk,rv->kv", flat, flat, precision=lax.Precision.HIGHEST), "grains")
    )
    basis = apply_inverse(flat, first_low)
    r_factor = first_low.T
    return (basis.reshape(slots, width, vectors), r_factor)


def solution(mesh):
    in_specs = (
        P("grains", None, None),
        P("grains", None, None, None),
        P("grains", None),
        P("grains"),
        P("grains", None, None),
    )
    out_specs = (P("grains", None, None), P())
    return jax.shard_map(local, mesh=mesh, in_specs=in_specs, out_specs=out_specs, check_vma=False)
```

profile of v0, /device:TPU:1, one launch (start us, length us, event | category | flops | bytes accessed | tf_op | source)
XLA Modules:
  0.0 348.2 jit_solution(11176043454755930773)
XLA Ops:
  7.9 0.8 fusion.4
  8.6 4.8 %fusion.6 = (bf16[64,128,128]{2,1,0:T(8,128)(2,1)S(1)}, f32[64,128,128]{2,1,0:T(8,128)}) fusion(f32[64,128,128]{2,1,0:T(8,128)} %param.5, f32[64]{0:T(128)S(1)} %compare_convert_fusion), kind=kLoop, calls=%fused_computation.40 | loop fusion | flops 2097152 | bytes 10486016 | tf_op jit(solution)/shard_map/convert_element_type | solution.py:23
  14.1 2.7 collective-permute-start
  16.9 1.4 gather_fusion.1
  18.5 5.6 %copy.17 = f32[64,128,128]{1,2,0:T(8,128)} copy(f32[64,128,128]{2,1,0:T(8,128)} %get-tuple-element.7) | data formatting | bytes 8388608 | tf_op jit(solution)/shard_map/mul | solution.py:21
  24.1 0.8 copy-done.3
  24.9 2.5 collective-permute-done.1
  27.4 2.1 pad_maximum_fusion
  29.5 13.9 %gather_fusion.2 = bf16[512,128,128]{2,1,0:T(8,128)(2,1)} fusion(bf16[96,128,128]{2,1,0:T(8,128)(2,1)S(1)} %pad_maximum_fusion, s32[1024]{0:T(1024)S(1)} %pad_clamp_fusion), kind=kCustom, calls=%fused_computation.2 | custom fusion | bytes 33556480 | tf_op jit(solution)/shard_map/gather | solution.py:29
  43.4 15.8 %fusion.7 = (bf16[64,128,128]{1,2,0:T(8,128)(2,1)S(1)}, f32[64,128,128]{1,2,0:T(8,128)}) fusion(f32[64,128,128]{1,2,0:T(8,128)} %copy.17, f32[64]{0:T(128)S(1)} %compare_convert_fusion, bf16[64,8,128,128]{3,2,1,0:T(8,128)(2,1)} %bitcast.59, bf16[64,8,128,128]{3,2,1,0:T(8,128)(2,1)} %param.6), kind=kOutput, calls=%fused_computation.41 | convolution fusion | flops 2150629376 | bytes 44040448 | tf_op jit(solution)/shard_map/bkij,bkjv->biv/dot_general | solution.py:30
  59.9 0.6 gather_fusion.3
  60.6 5.1 %collective-permute-start.3 = (bf16[16,128,128]{1,2,0:T(8,128)(2,1)S(1)}, bf16[16,128,128]{1,2,0:T(8,128)(2,1)S(1)}, u32[]{:S(2)}, u32[]{:S(2)}) collective-permute-start(bf16[16,128,128]{1,2,0:T(8,128)(2,1)S(1)} %gather_fusion.4), channel_id=1, source_target_pairs={{0,127},{1,0},{2,1},{3,2},{4,3},{5,4},{6,5},{7,6},{8,7},{9,8},{10,... | collective-permute-start | bytes 1572872 | tf_op jit(solution)/shard_map/ppermute | solution.py:11
  65.8 1.1 collective-permute-done.2
  66.9 2.6 collective-permute-done.3
  69.5 1.8 pad_maximum_fusion.1
  71.3 13.9 %gather_fusion.5 = bf16[512,128,128]{1,2,0:T(8,128)(2,1)} fusion(bf16[96,128,128]{1,2,0:T(8,128)(2,1)S(1)} %pad_maximum_fusion.1, s32[1024]{0:T(1024)S(1)} %pad_clamp_fusion), kind=kCustom, calls=%fused_computation.5 | custom fusion | bytes 33556480 | tf_op jit(solution)/shard_map/gather | solution.py:29
  85.2 15.6 %fusion.8 = (bf16[64,128,128]{1,2,0:T(8,128)(2,1)S(1)}, f32[64,128,128]{1,2,0:T(8,128)}) fusion(f32[64,128,128]{1,2,0:T(8,128)} %get-tuple-element.13, f32[64]{0:T(128)S(1)} %compare_convert_fusion, bf16[64,8,128,128]{2,3,1,0:T(8,128)(2,1)} %bitcast.60, bf16[64,8,128,128]{3,2,1,0:T(8,128)(2,1)} %param.6), kind=kOutput, calls=%fused_computation.42 | convolution fusion | flops 2150629376 | bytes 44040448 | tf_op jit(solution)/shard_map/bkij,bkjv->biv/dot_general | solution.py:30
  101.5 0.6 gather_fusion.6
  102.2 10.4 %collective-permute-start.5 = (bf16[16,128,128]{1,2,0:T(8,128)(2,1)S(1)}, bf16[16,128,128]{1,2,0:T(8,128)(2,1)S(1)}, u32[]{:S(2)}, u32[]{:S(2)}) collective-permute-start(bf16[16,128,128]{1,2,0:T(8,128)(2,1)S(1)} %gather_fusion.7), channel_id=1, source_target_pairs={{0,127},{1,0},{2,1},{3,2},{4,3},{5,4},{6,5},{7,6},{8,7},{9,8},{10,... | collective-permute-start | bytes 1572872 | tf_op jit(solution)/shard_map/ppermute | solution.py:11
  112.6 1.3 collective-permute-done.4
  114.1 1.8 pad_maximum_fusion.2
  115.9 13.9 %gather_fusion.8 = bf16[512,128,128]{1,2,0:T(8,128)(2,1)} fusion(bf16[96,128,128]{1,2,0:T(8,128)(2,1)S(1)} %pad_maximum_fusion.2, s32[1024]{0:T(1024)S(1)} %pad_clamp_fusion), kind=kCustom, calls=%fused_computation.8 | custom fusion | bytes 33556480 | tf_op jit(solution)/shard_map/gather | solution.py:29
  129.8 16.2 %bitcast_add_fusion = f32[64,128,128]{1,2,0:T(8,128)} fusion(f32[64,128,128]{1,2,0:T(8,128)} %get-tuple-element.15, bf16[64,8,128,128]{2,3,1,0:T(8,128)(2,1)} %bitcast.58, bf16[64,8,128,128]{3,2,1,0:T(8,128)(2,1)} %param.6, f32[64]{0:T(128)S(1)} %compare_convert_fusion), kind=kOutput, calls=%fused_computation.9 | convolution fusion | flops 2149580800 | bytes 41943296 | tf_op jit(solution)/shard_map/bkij,bkjv->biv/dot_general | solution.py:30
  146.0 7.6 %convolution_bitcast_fusion = f32[128,128]{0,1:T(8,128)} fusion(f32[64,128,128]{1,2,0:T(8,128)} %bitcast_add_fusion), kind=kOutput, calls=%fused_computation.19 | convolution fusion | flops 1610612736 | bytes 4259840 | tf_op jit(solution)/shard_map/rk,rv->kv/dot_general | solution.py:34
  153.6 152.3 %all-reduce.2.cloned.1.call-done = f32[128,128]{0,1:T(8,128)} async-done(((f32[128,128]{0,1:T(8,128)}), f32[128,128]{0,1:T(8,128)}) %all-reduce.2.cloned.1.call-update) | async-done | bytes 65552 | tf_op jit(solution)/shard_map/psum | solution.py:34
  305.9 0.9 copy.20
  306.9 0.9 fusion.2
  307.7 11.7 %cholesky.16 = f32[128,128]{1,0:T(8,128)S(1)} custom-call(f32[128,128]{1,0:T(8,128)S(1)} %fusion.2), custom_call_target="Cholesky" | custom-call | tf_op jit(solution)/shard_map/jit(cholesky)/cholesky | solution.py:33
  320.1 0.7 fusion.3
  320.8 0.7 copy.23
  321.5 9.8 %custom-call.6 = f32[1,128,128]{1,2,0:T(8,128)S(1)} custom-call(f32[1,128,128]{2,1,0:T(8,128)S(1)} %get-tuple-element.9), custom_call_target="InvertDiagBlocksLowerTriangular" | custom-call | tf_op jit(solution)/shard_map/triangular_solve | solution.py:15
  331.3 10.1 %fusion = f32[64,128,128]{2,1,0:T(8,128)} fusion(f32[64,128,128]{1,2,0:T(8,128)} %bitcast_add_fusion, f32[1,128,128]{1,2,0:T(8,128)S(1)} %custom-call.6), kind=kOutput, calls=%fused_computation.20 | convolution fusion | flops 1610612736 | bytes 8454144 | tf_op jit(solution)/shard_map/triangular_solve | solution.py:15
  (28 shorter events, 3.3 us)
Async XLA Ops:
  7.2 298.8 %all-reduce.2.cloned.1.call-start = ((), (), s32[]{:S(2)}) async-start(), calls=%async_computation | async-start | bytes 131072 | tf_op jit(solution)/shard_map/psum | solution.py:34
  8.6 9.6 %copy-start.4 = (s32[64,8]{0,1:T(8,128)S(1)}, s32[64,8]{0,1:T(8,128)}, u32[]{:S(2)}) copy-start(s32[64,8]{0,1:T(8,128)} %param.7) | copy-start | bytes 6148
  13.5 10.6 %copy-start.2 = (bf16[64,128,128]{2,1,0:T(8,128)(2,1)}, bf16[64,128,128]{2,1,0:T(8,128)(2,1)S(1)}, u32[]{:S(2)}) copy-start(bf16[64,128,128]{2,1,0:T(8,128)(2,1)S(1)} %get-tuple-element.6) | copy-start | bytes 6291460
  14.1 10.0 %collective-permute-start = (bf16[16,128,128]{2,1,0:T(8,128)(2,1)S(1)}, bf16[16,128,128]{2,1,0:T(8,128)(2,1)S(1)}, u32[]{:S(2)}, u32[]{:S(2)}) collective-permute-start(bf16[16,128,128]{2,1,0:T(8,128)(2,1)S(1)} %gather_fusion), channel_id=1, source_target_pairs={{0,1},{1,2},{2,3},{3,4},{4,5},{5,6},{6,7},{7,8},{8,9},{9,10},{10,1... | collective-permute-start | bytes 1572872 | tf_op jit(solution)/shard_map/ppermute | solution.py:11
  18.3 9.1 %collective-permute-start.1 = (bf16[16,128,128]{2,1,0:T(8,128)(2,1)}, bf16[16,128,128]{2,1,0:T(8,128)(2,1)}, u32[]{:S(2)}, u32[]{:S(2)}) collective-permute-start(bf16[16,128,128]{2,1,0:T(8,128)(2,1)} %gather_fusion.1), channel_id=1, source_target_pairs={{0,127},{1,0},{2,1},{3,2},{4,3},{5,4},{6,5},{7,6},{8,7},{9,8},{10,... | collective-permute-start | bytes 1572872 | tf_op jit(solution)/shard_map/ppermute | solution.py:11
  24.1 0.8 copy-start.3
  59.3 7.7 %copy-start = (bf16[64,128,128]{1,2,0:T(8,128)(2,1)}, bf16[64,128,128]{1,2,0:T(8,128)(2,1)S(1)}, u32[]{:S(2)}) copy-start(bf16[64,128,128]{1,2,0:T(8,128)(2,1)S(1)} %get-tuple-element.12) | copy-start | bytes 6291460
  60.6 6.4 %collective-permute-start.2 = (bf16[16,128,128]{1,2,0:T(8,128)(2,1)S(1)}, bf16[16,128,128]{1,2,0:T(8,128)(2,1)S(1)}, u32[]{:S(2)}, u32[]{:S(2)}) collective-permute-start(bf16[16,128,128]{1,2,0:T(8,128)(2,1)S(1)} %gather_fusion.3), channel_id=1, source_target_pairs={{0,1},{1,2},{2,3},{3,4},{4,5},{5,6},{6,7},{7,8},{8,9},{9,10},{10,1... | collective-permute-start | bytes 1572872 | tf_op jit(solution)/shard_map/ppermute | solution.py:11
  60.6 8.9 %collective-permute-start.3 = (bf16[16,128,128]{1,2,0:T(8,128)(2,1)S(1)}, bf16[16,128,128]{1,2,0:T(8,128)(2,1)S(1)}, u32[]{:S(2)}, u32[]{:S(2)}) collective-permute-start(bf16[16,128,128]{1,2,0:T(8,128)(2,1)S(1)} %gather_fusion.4), channel_id=1, source_target_pairs={{0,127},{1,0},{2,1},{3,2},{4,3},{5,4},{6,5},{7,6},{8,7},{9,8},{10,... | collective-permute-start | bytes 1572872 | tf_op jit(solution)/shard_map/ppermute | solution.py:11
  100.8 13.1 %copy-start.1 = (bf16[64,128,128]{1,2,0:T(8,128)(2,1)}, bf16[64,128,128]{1,2,0:T(8,128)(2,1)S(1)}, u32[]{:S(2)}) copy-start(bf16[64,128,128]{1,2,0:T(8,128)(2,1)S(1)} %get-tuple-element.14) | copy-start | bytes 6291460
  102.1 11.8 %collective-permute-start.4 = (bf16[16,128,128]{1,2,0:T(8,128)(2,1)S(1)}, bf16[16,128,128]{1,2,0:T(8,128)(2,1)S(1)}, u32[]{:S(2)}, u32[]{:S(2)}) collective-permute-start(bf16[16,128,128]{1,2,0:T(8,128)(2,1)S(1)} %gather_fusion.6), channel_id=1, source_target_pairs={{0,1},{1,2},{2,3},{3,4},{4,5},{5,6},{6,7},{7,8},{8,9},{9,10},{10,1... | collective-permute-start | bytes 1572872 | tf_op jit(solution)/shard_map/ppermute | solution.py:11
  102.2 11.9 %collective-permute-start.5 = (bf16[16,128,128]{1,2,0:T(8,128)(2,1)S(1)}, bf16[16,128,128]{1,2,0:T(8,128)(2,1)S(1)}, u32[]{:S(2)}, u32[]{:S(2)}) collective-permute-start(bf16[16,128,128]{1,2,0:T(8,128)(2,1)S(1)} %gather_fusion.7), channel_id=1, source_target_pairs={{0,127},{1,0},{2,1},{3,2},{4,3},{5,4},{6,5},{7,6},{8,7},{9,8},{10,... | collective-permute-start | bytes 1572872 | tf_op jit(solution)/shard_map/ppermute | solution.py:11
Sparse Core Ops, SparseCore 0:
  153.7 152.1 all-reduce.1
where the time goes:
time: 349 us; the launch traced here: 348 us
  waiting for transfers between devices  160 us (46%)
  matrix products  65.3 us (19%)
  local copies, waits for them, and re-layouts  54.7 us (16%)
  other arithmetic  34.9 us (10%)
  starting transfers between devices  18.4 us (5%)
  between operations  14.8 us (4%)
    psum x1, waiting for transfers between devices, local(): lax.psum(jnp.einsum('rk,rv->kv', flat, flat, precision=lax.Precision.HIGH...  152 us
    dot_general x3, matrix products, local(): jnp.einsum('bkij,bkjv->biv', blocks, gathered, preferred_element_type=jnp...  47.6 us
    gather x3, local copies, waits for them, and re-layouts, local(): gathered = extended[columns]  41.8 us
    ppermute x6, starting transfers between devices, passed_along(): lax.ppermute(shard, axis, [(i, (i + by) % length) for i in range(length)])  18.4 us
    another operation x3, other arithmetic, local(): jnp.linalg.cholesky(lax.psum(jnp.einsum('rk,rv->kv', flat, flat, precisio...  12.4 us
    another operation x1, matrix products, apply_inverse(): lax.linalg.triangular_solve(lower, matrix, left_side=False, lower=True, t...  10.1 us
    another operation x1, other arithmetic, apply_inverse(): lax.linalg.triangular_solve(lower, matrix, left_side=False, lower=True, t...  9.81 us
    ppermute x6, waiting for transfers between devices, passed_along(): lax.ppermute(shard, axis, [(i, (i + by) % length) for i in range(length)])  7.74 us
  transfers between devices with their start and end apart: 7, of which 6 were waited for; matrix products, arithmetic and copies ran while one was open for 2% of the time, Pallas kernels for 0%

commit v1 on v0

--- a/solution.py
+++ b/solution.py
@@ -31,7 +31,12 @@
         state = state + update * live
     flat = state.reshape(slots * width, vectors)
     first_low = jnp.linalg.cholesky(
-        lax.psum(jnp.einsum("rk,rv->kv", flat, flat, precision=lax.Precision.HIGHEST), "grains")
+        jnp.sum(
+            lax.all_gather(
+                jnp.einsum("rk,rv->kv", flat, flat, precision=lax.Precision.HIGHEST), "grains"
+            ),
+            axis=0,
+        )
     )
     basis = apply_inverse(flat, first_low)
     r_factor = first_low.T

time: 349 us -> 281 us (0.81)
  waiting for transfers between devices: 160 us -> 90.4 us
    psum x1 -> x0, waiting for transfers between devices: 152 us -> none  [local(): lax.psum(jnp.einsum('rk,rv->kv', flat, flat, precision=lax.Precision.HIGH...]
    all_gather x0 -> x1, waiting for transfers between devices: none -> 82.7 us  [local(): lax.all_gather(jnp.einsum('rk,rv->kv', flat, flat, precision=lax.Precisio...]
    reduce_sum x0 -> x1, other arithmetic: none -> 3.81 us  [local(): jnp.sum(lax.all_gather(jnp.einsum('rk,rv->kv', flat, flat, precision=lax....]
  transfers between devices with their start and end apart: 7 -> 7, of which waited for: 6 -> 6; matrix products, arithmetic and copies ran while one was open for 2% -> 3% of each run, Pallas kernels for 0% -> 0%
where the time goes in v1:
time: 281 us
  waiting for transfers between devices  90.4 us (32%)
  matrix products  65.3 us (23%)
  local copies, waits for them, and re-layouts  53.8 us (19%)
  other arithmetic  37.9 us (13%)
  starting transfers between devices  18.4 us (7%)
  between operations  14.8 us (5%)
    all_gather x1, waiting for transfers between devices, local(): lax.all_gather(jnp.einsum('rk,rv->kv', flat, flat, precision=lax.Precisio...  82.7 us
    dot_general x3, matrix products, local(): jnp.einsum('bkij,bkjv->biv', blocks, gathered, preferred_element_type=jnp...  47.6 us
    gather x3, local copies, waits for them, and re-layouts, local(): gathered = extended[columns]  41.8 us
    ppermute x6, starting transfers between devices, passed_along(): lax.ppermute(shard, axis, [(i, (i + by) % length) for i in range(length)])  18.4 us
    another operation x3, other arithmetic, local(): jnp.linalg.cholesky(jnp.sum(lax.all_gather(jnp.einsum('rk,rv->kv', flat,...  12.4 us
    another operation x1, matrix products, apply_inverse(): lax.linalg.triangular_solve(lower, matrix, left_side=False, lower=True, t...  10.1 us
    another operation x1, other arithmetic, apply_inverse(): lax.linalg.triangular_solve(lower, matrix, left_side=False, lower=True, t...  9.81 us
    ppermute x6, waiting for transfers between devices, passed_along(): lax.ppermute(shard, axis, [(i, (i + by) % length) for i in range(length)])  7.74 us
  transfers between devices with their start and end apart: 7, of which 6 were waited for; matrix products, arithmetic and copies ran while one was open for 3% of the time, Pallas kernels for 0%

profile of v1, /device:TPU:1, one launch (start us, length us, event | category | flops | bytes accessed | tf_op | source)
XLA Modules:
  0.0 280.7 jit_solution(1179201874221612051)
XLA Ops:
  7.9 0.8 fusion.4
  8.6 4.8 %fusion.6 = (bf16[64,128,128]{2,1,0:T(8,128)(2,1)S(1)}, f32[64,128,128]{2,1,0:T(8,128)}) fusion(f32[64,128,128]{2,1,0:T(8,128)} %param.5, f32[64]{0:T(128)S(1)} %compare_convert_fusion), kind=kLoop, calls=%fused_computation.40 | loop fusion | flops 2097152 | bytes 10486016 | tf_op jit(solution)/shard_map/convert_element_type | solution.py:23
  14.1 2.7 collective-permute-start
  16.9 1.4 gather_fusion.1
  18.5 5.6 %copy.24 = f32[64,128,128]{1,2,0:T(8,128)} copy(f32[64,128,128]{2,1,0:T(8,128)} %get-tuple-element.9) | data formatting | bytes 8388608 | tf_op jit(solution)/shard_map/mul | solution.py:21
  24.1 0.8 copy-done.3
  24.9 2.5 collective-permute-done.1
  27.4 2.1 pad_maximum_fusion
  29.5 13.9 %gather_fusion.2 = bf16[512,128,128]{2,1,0:T(8,128)(2,1)} fusion(bf16[96,128,128]{2,1,0:T(8,128)(2,1)S(1)} %pad_maximum_fusion, s32[1024]{0:T(1024)S(1)} %pad_clamp_fusion), kind=kCustom, calls=%fused_computation.2 | custom fusion | bytes 33556480 | tf_op jit(solution)/shard_map/gather | solution.py:29
  43.4 15.8 %fusion.7 = (bf16[64,128,128]{1,2,0:T(8,128)(2,1)S(1)}, f32[64,128,128]{1,2,0:T(8,128)}) fusion(f32[64,128,128]{1,2,0:T(8,128)} %copy.24, f32[64]{0:T(128)S(1)} %compare_convert_fusion, bf16[64,8,128,128]{3,2,1,0:T(8,128)(2,1)} %bitcast.60, bf16[64,8,128,128]{3,2,1,0:T(8,128)(2,1)} %param.6), kind=kOutput, calls=%fused_computation.41 | convolution fusion | flops 2150629376 | bytes 44040448 | tf_op jit(solution)/shard_map/bkij,bkjv->biv/dot_general | solution.py:30
  59.3 0.6 gather_fusion.4
  59.9 0.6 gather_fusion.3
  60.6 5.1 %collective-permute-start.3 = (bf16[16,128,128]{1,2,0:T(8,128)(2,1)S(1)}, bf16[16,128,128]{1,2,0:T(8,128)(2,1)S(1)}, u32[]{:S(2)}, u32[]{:S(2)}) collective-permute-start(bf16[16,128,128]{1,2,0:T(8,128)(2,1)S(1)} %gather_fusion.4), channel_id=1, source_target_pairs={{0,127},{1,0},{2,1},{3,2},{4,3},{5,4},{6,5},{7,6},{8,7},{9,8},{10,... | collective-permute-start | bytes 1572872 | tf_op jit(solution)/shard_map/ppermute | solution.py:11
  65.8 1.1 collective-permute-done.2
  66.9 2.6 collective-permute-done.3
  69.5 1.8 pad_maximum_fusion.1
  71.3 13.9 %gather_fusion.5 = bf16[512,128,128]{1,2,0:T(8,128)(2,1)} fusion(bf16[96,128,128]{1,2,0:T(8,128)(2,1)S(1)} %pad_maximum_fusion.1, s32[1024]{0:T(1024)S(1)} %pad_clamp_fusion), kind=kCustom, calls=%fused_computation.5 | custom fusion | bytes 33556480 | tf_op jit(solution)/shard_map/gather | solution.py:29
  85.2 15.6 %fusion.8 = (bf16[64,128,128]{1,2,0:T(8,128)(2,1)S(1)}, f32[64,128,128]{1,2,0:T(8,128)}) fusion(f32[64,128,128]{1,2,0:T(8,128)} %get-tuple-element.15, f32[64]{0:T(128)S(1)} %compare_convert_fusion, bf16[64,8,128,128]{2,3,1,0:T(8,128)(2,1)} %bitcast.61, bf16[64,8,128,128]{3,2,1,0:T(8,128)(2,1)} %param.6), kind=kOutput, calls=%fused_computation.42 | convolution fusion | flops 2150629376 | bytes 44040448 | tf_op jit(solution)/shard_map/bkij,bkjv->biv/dot_general | solution.py:30
  101.5 0.6 gather_fusion.6
  102.2 10.4 %collective-permute-start.5 = (bf16[16,128,128]{1,2,0:T(8,128)(2,1)S(1)}, bf16[16,128,128]{1,2,0:T(8,128)(2,1)S(1)}, u32[]{:S(2)}, u32[]{:S(2)}) collective-permute-start(bf16[16,128,128]{1,2,0:T(8,128)(2,1)S(1)} %gather_fusion.7), channel_id=1, source_target_pairs={{0,127},{1,0},{2,1},{3,2},{4,3},{5,4},{6,5},{7,6},{8,7},{9,8},{10,... | collective-permute-start | bytes 1572872 | tf_op jit(solution)/shard_map/ppermute | solution.py:11
  112.6 1.3 collective-permute-done.4
  114.1 1.8 pad_maximum_fusion.2
  115.9 13.9 %gather_fusion.8 = bf16[512,128,128]{1,2,0:T(8,128)(2,1)} fusion(bf16[96,128,128]{1,2,0:T(8,128)(2,1)S(1)} %pad_maximum_fusion.2, s32[1024]{0:T(1024)S(1)} %pad_clamp_fusion), kind=kCustom, calls=%fused_computation.8 | custom fusion | bytes 33556480 | tf_op jit(solution)/shard_map/gather | solution.py:29
  129.8 16.2 %bitcast_add_fusion = f32[64,128,128]{1,2,0:T(8,128)} fusion(f32[64,128,128]{1,2,0:T(8,128)} %get-tuple-element.17, bf16[64,8,128,128]{2,3,1,0:T(8,128)(2,1)} %bitcast.59, bf16[64,8,128,128]{3,2,1,0:T(8,128)(2,1)} %param.6, f32[64]{0:T(128)S(1)} %compare_convert_fusion), kind=kOutput, calls=%fused_computation.9 | convolution fusion | flops 2149580800 | bytes 41943296 | tf_op jit(solution)/shard_map/bkij,bkjv->biv/dot_general | solution.py:30
  146.0 7.6 %convolution_bitcast_fusion = f32[128,128]{1,0:T(8,128)} fusion(f32[64,128,128]{1,2,0:T(8,128)} %bitcast_add_fusion), kind=kOutput, calls=%fused_computation.19 | convolution fusion | flops 1610612736 | bytes 4259840 | tf_op jit(solution)/shard_map/rk,rv->kv/dot_general | solution.py:36
  153.6 82.7 %all-gather.3.cloned.1.call-done = f32[16384,128]{1,0:T(8,128)} async-done(((f32[128,128]{1,0:T(8,128)}), f32[16384,128]{1,0:T(8,128)}) %all-gather.3.cloned.1.call-update) | async-done | bytes 8388624 | tf_op jit(solution)/shard_map/all_gather | solution.py:35
  236.2 3.8 %reduce_sum.9 = f32[128,128]{1,0:T(8,128)S(1)} reduce(f32[128,128,128]{2,1,0:T(8,128)} %bitcast.62, f32[]{:T(128)} %constant.45.clone.1), dimensions={0}, to_apply=%region_0.0 | reduce | flops 2080768 | bytes 8454148 | tf_op jit(solution)/shard_map/reduce_sum | solution.py:34
  240.2 11.7 %cholesky.16 = f32[128,128]{1,0:T(8,128)S(1)} custom-call(f32[128,128]{1,0:T(8,128)S(1)} %fusion.2), custom_call_target="Cholesky" | custom-call | tf_op jit(solution)/shard_map/jit(cholesky)/cholesky | solution.py:33
  252.6 0.7 fusion.3
  253.2 0.7 copy.29
  254.0 9.8 %custom-call.6 = f32[1,128,128]{1,2,0:T(8,128)S(1)} custom-call(f32[1,128,128]{2,1,0:T(8,128)S(1)} %get-tuple-element.11), custom_call_target="InvertDiagBlocksLowerTriangular" | custom-call | tf_op jit(solution)/shard_map/triangular_solve | solution.py:15
  263.8 10.1 %fusion = f32[64,128,128]{2,1,0:T(8,128)} fusion(f32[64,128,128]{1,2,0:T(8,128)} %bitcast_add_fusion, f32[1,128,128]{1,2,0:T(8,128)S(1)} %custom-call.6), kind=kOutput, calls=%fused_computation.20 | convolution fusion | flops 1610612736 | bytes 8454144 | tf_op jit(solution)/shard_map/triangular_solve | solution.py:15
  (29 shorter events, 2.7 us)
Async XLA Ops:
  7.2 229.1 %all-gather.3.cloned.1.call-start = ((), (), s32[]{:S(2)}) async-start(), calls=%async_computation | async-start | bytes 8454144 | tf_op jit(solution)/shard_map/all_gather | solution.py:35
  8.6 9.6 %copy-start.4 = (s32[64,8]{0,1:T(8,128)S(1)}, s32[64,8]{0,1:T(8,128)}, u32[]{:S(2)}) copy-start(s32[64,8]{0,1:T(8,128)} %param.7) | copy-start | bytes 6148
  13.5 10.6 %copy-start.2 = (bf16[64,128,128]{2,1,0:T(8,128)(2,1)}, bf16[64,128,128]{2,1,0:T(8,128)(2,1)S(1)}, u32[]{:S(2)}) copy-start(bf16[64,128,128]{2,1,0:T(8,128)(2,1)S(1)} %get-tuple-element.8) | copy-start | bytes 6291460
  14.1 10.0 %collective-permute-start = (bf16[16,128,128]{2,1,0:T(8,128)(2,1)S(1)}, bf16[16,128,128]{2,1,0:T(8,128)(2,1)S(1)}, u32[]{:S(2)}, u32[]{:S(2)}) collective-permute-start(bf16[16,128,128]{2,1,0:T(8,128)(2,1)S(1)} %gather_fusion), channel_id=1, source_target_pairs={{0,1},{1,2},{2,3},{3,4},{4,5},{5,6},{6,7},{7,8},{8,9},{9,10},{10,1... | collective-permute-start | bytes 1572872 | tf_op jit(solution)/shard_map/ppermute | solution.py:11
  18.3 9.1 %collective-permute-start.1 = (bf16[16,128,128]{2,1,0:T(8,128)(2,1)}, bf16[16,128,128]{2,1,0:T(8,128)(2,1)}, u32[]{:S(2)}, u32[]{:S(2)}) collective-permute-start(bf16[16,128,128]{2,1,0:T(8,128)(2,1)} %gather_fusion.1), channel_id=1, source_target_pairs={{0,127},{1,0},{2,1},{3,2},{4,3},{5,4},{6,5},{7,6},{8,7},{9,8},{10,... | collective-permute-start | bytes 1572872 | tf_op jit(solution)/shard_map/ppermute | solution.py:11
  24.1 0.8 copy-start.3
  59.3 7.7 %copy-start = (bf16[64,128,128]{1,2,0:T(8,128)(2,1)}, bf16[64,128,128]{1,2,0:T(8,128)(2,1)S(1)}, u32[]{:S(2)}) copy-start(bf16[64,128,128]{1,2,0:T(8,128)(2,1)S(1)} %get-tuple-element.14) | copy-start | bytes 6291460
  60.6 6.4 %collective-permute-start.2 = (bf16[16,128,128]{1,2,0:T(8,128)(2,1)S(1)}, bf16[16,128,128]{1,2,0:T(8,128)(2,1)S(1)}, u32[]{:S(2)}, u32[]{:S(2)}) collective-permute-start(bf16[16,128,128]{1,2,0:T(8,128)(2,1)S(1)} %gather_fusion.3), channel_id=1, source_target_pairs={{0,1},{1,2},{2,3},{3,4},{4,5},{5,6},{6,7},{7,8},{8,9},{9,10},{10,1... | collective-permute-start | bytes 1572872 | tf_op jit(solution)/shard_map/ppermute | solution.py:11
  60.6 8.9 %collective-permute-start.3 = (bf16[16,128,128]{1,2,0:T(8,128)(2,1)S(1)}, bf16[16,128,128]{1,2,0:T(8,128)(2,1)S(1)}, u32[]{:S(2)}, u32[]{:S(2)}) collective-permute-start(bf16[16,128,128]{1,2,0:T(8,128)(2,1)S(1)} %gather_fusion.4), channel_id=1, source_target_pairs={{0,127},{1,0},{2,1},{3,2},{4,3},{5,4},{6,5},{7,6},{8,7},{9,8},{10,... | collective-permute-start | bytes 1572872 | tf_op jit(solution)/shard_map/ppermute | solution.py:11
  100.8 13.1 %copy-start.1 = (bf16[64,128,128]{1,2,0:T(8,128)(2,1)}, bf16[64,128,128]{1,2,0:T(8,128)(2,1)S(1)}, u32[]{:S(2)}) copy-start(bf16[64,128,128]{1,2,0:T(8,128)(2,1)S(1)} %get-tuple-element.16) | copy-start | bytes 6291460
  102.1 11.8 %collective-permute-start.4 = (bf16[16,128,128]{1,2,0:T(8,128)(2,1)S(1)}, bf16[16,128,128]{1,2,0:T(8,128)(2,1)S(1)}, u32[]{:S(2)}, u32[]{:S(2)}) collective-permute-start(bf16[16,128,128]{1,2,0:T(8,128)(2,1)S(1)} %gather_fusion.6), channel_id=1, source_target_pairs={{0,1},{1,2},{2,3},{3,4},{4,5},{5,6},{6,7},{7,8},{8,9},{9,10},{10,1... | collective-permute-start | bytes 1572872 | tf_op jit(solution)/shard_map/ppermute | solution.py:11
  102.2 11.9 %collective-permute-start.5 = (bf16[16,128,128]{1,2,0:T(8,128)(2,1)S(1)}, bf16[16,128,128]{1,2,0:T(8,128)(2,1)S(1)}, u32[]{:S(2)}, u32[]{:S(2)}) collective-permute-start(bf16[16,128,128]{1,2,0:T(8,128)(2,1)S(1)} %gather_fusion.7), channel_id=1, source_target_pairs={{0,127},{1,0},{2,1},{3,2},{4,3},{5,4},{6,5},{7,6},{8,7},{9,8},{10,... | collective-permute-start | bytes 1572872 | tf_op jit(solution)/shard_map/ppermute | solution.py:11
Sparse Core Ops, SparseCore 0:
  153.7 82.5 all-gather.2
